TPU v7x, 256 devices: a whole 4x4x8 slice. The times are simulated.
256 devices in a mesh: row: 16 (over y_lo, x, core), col: 16 (over y_hi, z).
Axes of the slice: x: 4, y: 4 (y_hi: 2, y_lo: 2; y = y_hi * 2 + y_lo), z: 8, core: 2. Of those that a mesh axis runs over, the one named last changes fastest.
Arguments:
- tiles: bfloat16 [16, 16, 128, 128, 128], P('row', 'col'), as said below
- coords: int32 [16, 16, 2, 128], P('row', 'col'), may hold values from 0 to 63, as said below
- counts: int32 [16, 16], P('row', 'col'), may hold values from 1 to 128, as said below
- valid: int32 [131072], P(('row', 'col')), may hold values 0 or 1
- start: float32 [8, 131072], P(None, ('row', 'col'))
- rotations: float32 [2, 8, 24], replicated, as said below
Outputs:
- eigenmaps: float32 [8, 131072], P(None, ('row', 'col'))
- ritz: float32 [8, 8], replicated
Inputs may be any that keep to these rules, and one draw needn't show every extreme that they name: coords[r, c, 0, s] is a block row from 0 to 63 and coords[r, c, 1, s] a block column from 0 to 63; the live slots of one owner name distinct blocks, each on or above the block diagonal (g_row <= g_col). The live slots of an owner are the first counts[r, c] of its list; one owner in grid row 0 has all 128 live. `tiles`: nonnegative; a tile on the block diagonal is symmetric. The Rayleigh-Ritz coefficients of the current vectors, rotations[t, :, 0 to 7], form a matrix whose diagonal dominates its rows.
All inputs are finite; a program needn't handle non-finite values. No bound on the sum of `valid` on one device may be relied on, other than what follows from the above.
Results may differ from a plain program's by a relative error of at most 0.0013.
Values may be sent and summed in bfloat16 or wider, within the bound.
No kernel may reach another device: no remote copies, remote signals or barrier semaphores. Data moves between devices by JAX's collectives and lax.ppermute only.
A program may use at most 64 MiB of HBM per device.

v0:
```python
import jax
import jax.numpy as jnp
from jax import lax
from jax.sharding import PartitionSpec as P


def matmul_high(left, right):
    return jnp.dot(left, right, precision=lax.Precision.HIGHEST)


def lower_inverse(lower_factor):
    order_size = lower_factor.shape[0]
    identity = jnp.eye(order_size, dtype=lower_factor.dtype)
    inverse_rows = []
    for row_at in range(order_size):
        partial_row = identity[row_at]
        for prior_at in range(row_at):
            partial_row = partial_row - lower_factor[row_at, prior_at] * inverse_rows[prior_at]
        inverse_rows.append(partial_row / lower_factor[row_at, row_at])
    return jnp.stack(inverse_rows)


def settle(new_vecs, new_images, new_steps, step_images, gram_x, gram_ax, node_total):
    lower_factor = jnp.linalg.cholesky(gram_x / node_total)
    inverse = lower_inverse(lower_factor)
    theta = matmul_high(matmul_high(inverse, gram_ax / node_total), inverse.T)
    return (
        matmul_high(inverse, new_vecs),
        matmul_high(inverse, new_images),
        matmul_high(inverse, new_steps),
        matmul_high(inverse, step_images),
        theta,
    )


def gram_sums(new_vecs, new_images):
    return lax.psum(
        (matmul_high(new_vecs, new_vecs.T), matmul_high(new_images, new_vecs.T)), ("row", "col")
    )


def local_terms(
    part_tiles, part_rows, part_cols, weight_direct, weight_mirror, col_blocks, row_blocks
):
    row_span = row_blocks.shape[1]
    col_span = col_blocks.shape[1]
    col_values = jnp.take(col_blocks, part_cols, axis=1)
    row_values = jnp.take(row_blocks, part_rows, axis=1)
    direct = (
        jnp.einsum("sut,cst->csu", part_tiles, col_values, preferred_element_type=jnp.float32)
        * weight_direct[None, :, None]
    )
    mirror = (
        jnp.einsum("sut,csu->cst", part_tiles, row_values, preferred_element_type=jnp.float32)
        * weight_mirror[None, :, None]
    )
    pick_rows = (part_rows[:, None] == jnp.arange(row_span, dtype=jnp.int32)[None, :]).astype(
        jnp.float32
    )
    pick_cols = (part_cols[:, None] == jnp.arange(col_span, dtype=jnp.int32)[None, :]).astype(
        jnp.float32
    )
    rows_sum = jnp.einsum("sp,csu->cpu", pick_rows, direct, precision=lax.Precision.HIGHEST)
    cols_sum = jnp.einsum("sq,cst->cqt", pick_cols, mirror, precision=lax.Precision.HIGHEST)
    return (rows_sum, cols_sum)


def body(tiles, coords, counts, valid, start, rotations):
    row_count = lax.axis_size("row")
    col_count = lax.axis_size("col")
    row_index = lax.axis_index("row")
    col_index = lax.axis_index("col")
    slot_count = tiles.shape[2]
    tile_side = tiles.shape[3]
    stretch_nodes = valid.shape[0]
    per_stretch = stretch_nodes // tile_side
    row_span = col_count * per_stretch
    col_span = row_count * per_stretch
    node_total = jnp.float32(stretch_nodes * row_count * col_count)
    vec_count = start.shape[0]
    flat_tiles = tiles.reshape(slot_count, tile_side, tile_side)
    block_rows = coords[0, 0, 0]
    block_cols = coords[0, 0, 1]
    live_count = counts[0, 0]
    global_rows = row_index * row_span + block_rows
    global_cols = (
        block_cols // per_stretch * col_count + col_index
    ) * per_stretch + block_cols % per_stretch
    live = (jnp.arange(slot_count, dtype=jnp.int32) < live_count).astype(jnp.float32)
    mirror_weight = live * (global_rows != global_cols).astype(jnp.float32)

    def graph_product(vectors):
        width = vectors.shape[0]
        short = vectors.astype(jnp.bfloat16)
        col_side = lax.all_gather(short, "row", axis=1, tiled=True)
        row_side = lax.all_gather(short, "col", axis=1, tiled=True)
        col_blocks = col_side.reshape(width, col_span, tile_side)
        row_blocks = row_side.reshape(width, row_span, tile_side)
        rows_total, cols_total = local_terms(
            flat_tiles, block_rows, block_cols, live, mirror_weight, col_blocks, row_blocks
        )
        direct_part = lax.psum_scatter(
            rows_total.reshape(width, row_span * tile_side), "col", scatter_dimension=1, tiled=True
        )
        mirror_part = lax.psum_scatter(
            cols_total.reshape(width, col_span * tile_side), "row", scatter_dimension=1, tiled=True
        )
        return direct_part + mirror_part

    node_mask = valid.astype(jnp.float32)
    first_vecs = start * node_mask[None, :]
    raw = graph_product(jnp.concatenate([node_mask[None, :], first_vecs], 0))
    degree = raw[0]
    first_images = node_mask[None, :] * (degree[None, :] * first_vecs - raw[1:])
    zero_steps = jnp.zeros_like(first_vecs)
    gram_x, gram_ax = gram_sums(first_vecs, first_images)
    vecs, images, steps, step_images, theta = settle(
        first_vecs, first_images, zero_steps, zero_steps, gram_x, gram_ax, node_total
    )
    for turn in range(rotations.shape[0]):
        resid = images - matmul_high(theta, vecs)
        resid_images = node_mask[None, :] * (degree[None, :] * resid - graph_product(resid))
        stacked = jnp.concatenate([vecs, resid, steps], 0)
        stacked_images = jnp.concatenate([images, resid_images, step_images], 0)
        rotation = rotations[turn]
        new_vecs = matmul_high(rotation, stacked)
        new_images = matmul_high(rotation, stacked_images)
        gram_x, gram_ax = gram_sums(new_vecs, new_images)
        new_steps = matmul_high(rotation[:, vec_count:], stacked[vec_count:])
        new_step_images = matmul_high(rotation[:, vec_count:], stacked_images[vec_count:])
        vecs, images, steps, step_images, theta = settle(
            new_vecs, new_images, new_steps, new_step_images, gram_x, gram_ax, node_total
        )
    return (vecs, theta)


def solution(mesh):
    in_specs = (
        P("row", "col", None, None, None),
        P("row", "col", None, None),
        P("row", "col"),
        P(("row", "col")),
        P(None, ("row", "col")),
        P(),
    )
    out_specs = (P(None, ("row", "col")), P())
    return jax.shard_map(body, mesh=mesh, in_specs=in_specs, out_specs=out_specs, check_vma=False)
```

profile of v0, /device:TPU:1, one launch (start us, length us, event | category | flops | bytes accessed | tf_op | source)
XLA Modules:
  0.0 1272.5 jit_solution(13226586753436208169)
XLA Ops:
  7.2 0.8 compare_and_fusion
  8.0 0.8 slice_bitcast_fusion.2
  8.8 0.7 convert_convert_fusion
  9.5 0.7 multiply_convert_fusion
  10.2 39.4 %all_gather.19 = bf16[9,8192]{1,0:T(8,128)(2,1)S(1)} all-gather(bf16[9,512]{1,0:T(8,128)(2,1)S(1)} %pad_maximum_fusion.8), channel_id=1, replica_groups=mesh['row'=16,'col'=16] {'col'}, dimensions={1}, use_global_device_ids=true | all-gather | bytes 156672 | tf_op jit(solution)/shard_map/all_gather | solution.py:96
  50.5 0.7 gather_fusion.1
  51.2 3.4 fusion.8
  55.3 1.1 copy.34
  56.4 26.8 %all_gather.18 = bf16[9,8192]{1,0:T(8,128)(2,1)S(1)} all-gather(bf16[9,512]{1,0:T(8,128)(2,1)S(1)} %pad_maximum_fusion.8), channel_id=1, replica_groups=mesh['row'=16,'col'=16] {'row'}, dimensions={1}, use_global_device_ids=true | all-gather | bytes 156672 | tf_op jit(solution)/shard_map/all_gather | solution.py:95
  83.4 0.7 gather_fusion
  84.2 4.5 fusion.10
  88.7 0.5 convolution_bitcast_fusion.1
  89.3 1.1 copy.32
  90.7 26.8 %reduce-scatter.9.cloned.1.call-done = f32[9,512]{1,0:T(8,128)} async-done(((f32[9,8192]{1,0:T(8,128)}), f32[9,512]{1,0:T(8,128)}) %reduce-scatter.9.cloned.1.call-update) | async-done | bytes 18448 | tf_op jit(solution)/shard_map/reduce_scatter | solution.py:105
  117.5 198.7 %reduce-scatter.7.cloned.1.call-done = f32[9,512]{1,0:T(8,128)} async-done(((f32[9,8192]{1,0:T(8,128)}), f32[9,512]{1,0:T(8,128)}) %reduce-scatter.7.cloned.1.call-update) | async-done | bytes 18448 | tf_op jit(solution)/shard_map/reduce_scatter | solution.py:102
  316.2 0.8 add.100
  317.1 79.7 %all-reduce.2 = (f32[8,8]{0,1:T(8,128)S(1)}, f32[8,8]{0,1:T(8,128)S(1)}) all-reduce(f32[8,8]{0,1:T(8,128)S(1)} %fusion.95, f32[8,8]{0,1:T(8,128)S(1)} %fusion.87), channel_id=1, replica_groups=mesh['row'=16,'col'=16] {'row','col'}, use_global_device_ids=true, to_apply=%region_0.1 | all-reduce | flops 128 | bytes 1024 | tf_op jit(solution)/shard_map/psum | solution.py:37
  396.9 0.7 cholesky.59
  397.6 0.6 compare_reduce_fusion.2
  398.3 0.6 fusion.110
  398.9 0.7 fusion.147
  399.6 0.7 fusion.148
  400.4 22.6 %subtract_divide_fusion.14 = (f32[1,8]{1,0:T(1,128)S(1)}, f32[1,8]{1,0:T(1,128)S(1)}, f32[1,8]{1,0:T(1,128)S(1)}, f32[1,8]{1,0:T(1,128)S(1)}, f32[1,8]{1,0:T(1,1...) fusion(f32[]{:T(128)} %bitcast.36, f32[]{:T(128)} %bitcast.35, f32[]{:T(128)} %bitcast.34, ...), kind=kLoop, calls=%fused_computation.199 | loop fusion | flops 512 | bytes 656 | tf_op jit(solution)/shard_map/div | solution.py:19
  423.7 31.8 %all_gather.21 = bf16[8,8192]{1,0:T(8,128)(2,1)S(1)} all-gather(bf16[8,512]{1,0:T(8,128)(2,1)S(1)} %get-tuple-element.153), channel_id=1, replica_groups=mesh['row'=16,'col'=16] {'col'}, dimensions={1}, use_global_device_ids=true | all-gather | bytes 139264 | tf_op jit(solution)/shard_map/all_gather | solution.py:96
  455.4 24.9 %all_gather.20 = bf16[8,8192]{1,0:T(8,128)(2,1)S(1)} all-gather(bf16[8,512]{1,0:T(8,128)(2,1)S(1)} %get-tuple-element.153), channel_id=1, replica_groups=mesh['row'=16,'col'=16] {'row'}, dimensions={1}, use_global_device_ids=true | all-gather | bytes 139264 | tf_op jit(solution)/shard_map/all_gather | solution.py:95
  480.4 0.7 gather_fusion.3
  481.1 3.4 fusion.4
  485.0 0.8 copy.69
  485.9 0.7 gather_fusion.2
  486.6 4.5 fusion.6
  491.5 0.9 copy.70
  492.9 0.6 fusion.68
  493.5 45.7 %reduce-scatter.13.cloned.1.call-done = f32[8,512]{1,0:T(8,128)} async-done(((f32[8,8192]{1,0:T(8,128)}), f32[8,512]{1,0:T(8,128)}) %reduce-scatter.13.cloned.1.call-update) | async-done | bytes 16400 | tf_op jit(solution)/shard_map/reduce_scatter | solution.py:105
  539.2 197.1 %reduce-scatter.11.cloned.1.call-done = f32[8,512]{1,0:T(8,128)} async-done(((f32[8,8192]{1,0:T(8,128)}), f32[8,512]{1,0:T(8,128)}) %reduce-scatter.11.cloned.1.call-update) | async-done | bytes 16400 | tf_op jit(solution)/shard_map/reduce_scatter | solution.py:102
  736.3 0.7 subtract_multiply_fusion.1
  737.3 79.8 %all-reduce.1 = (f32[8,8]{0,1:T(8,128)S(1)}, f32[8,8]{0,1:T(8,128)S(1)}) all-reduce(f32[8,8]{0,1:T(8,128)S(1)} %fusion.152, f32[8,8]{0,1:T(8,128)S(1)} %fusion.155), channel_id=1, replica_groups=mesh['row'=16,'col'=16] {'row','col'}, use_global_device_ids=true, to_apply=%region_6.9 | all-reduce | flops 128 | bytes 1024 | tf_op jit(solution)/shard_map/psum | solution.py:37
  817.2 0.7 cholesky.70
  817.9 0.6 compare_reduce_fusion.1
  818.6 0.6 fusion.111
  819.2 0.7 fusion.145
  820.0 0.7 fusion.146
  820.7 22.6 %subtract_divide_fusion.7 = (f32[1,8]{1,0:T(1,128)S(1)}, f32[1,8]{1,0:T(1,128)S(1)}, f32[1,8]{1,0:T(1,128)S(1)}, f32[1,8]{1,0:T(1,128)S(1)}, f32[1,8]{1,0:T(1,12...) fusion(f32[]{:T(128)} %bitcast.87, f32[]{:T(128)} %bitcast.86, f32[]{:T(128)} %bitcast.85, ...), kind=kLoop, calls=%fused_computation.190 | loop fusion | flops 512 | bytes 656 | tf_op jit(solution)/shard_map/div | solution.py:19
  844.0 31.8 %all_gather.23 = bf16[8,8192]{1,0:T(8,128)(2,1)S(1)} all-gather(bf16[8,512]{1,0:T(8,128)(2,1)S(1)} %get-tuple-element.155), channel_id=1, replica_groups=mesh['row'=16,'col'=16] {'col'}, dimensions={1}, use_global_device_ids=true | all-gather | bytes 139264 | tf_op jit(solution)/shard_map/all_gather | solution.py:96
  875.8 24.9 %all_gather.22 = bf16[8,8192]{1,0:T(8,128)(2,1)S(1)} all-gather(bf16[8,512]{1,0:T(8,128)(2,1)S(1)} %get-tuple-element.155), channel_id=1, replica_groups=mesh['row'=16,'col'=16] {'row'}, dimensions={1}, use_global_device_ids=true | all-gather | bytes 139264 | tf_op jit(solution)/shard_map/all_gather | solution.py:95
  900.7 0.7 gather_fusion.5
  901.4 3.4 fusion
  905.3 0.8 copy.67
  906.3 0.7 gather_fusion.4
  906.9 4.5 fusion.2
  911.9 0.9 copy.68
  913.4 0.6 fusion.69
  914.3 45.1 %reduce-scatter.17.cloned.1.call-done = f32[8,512]{1,0:T(8,128)} async-done(((f32[8,8192]{1,0:T(8,128)}), f32[8,512]{1,0:T(8,128)}) %reduce-scatter.17.cloned.1.call-update) | async-done | bytes 16400 | tf_op jit(solution)/shard_map/reduce_scatter | solution.py:105
  959.4 197.2 %reduce-scatter.15.cloned.1.call-done = f32[8,512]{1,0:T(8,128)} async-done(((f32[8,8192]{1,0:T(8,128)}), f32[8,512]{1,0:T(8,128)}) %reduce-scatter.15.cloned.1.call-update) | async-done | bytes 16400 | tf_op jit(solution)/shard_map/reduce_scatter | solution.py:102
  1156.6 0.7 subtract_multiply_fusion
  1157.3 0.6 fusion.62
  1158.2 79.7 %all-reduce = (f32[8,8]{0,1:T(8,128)S(1)}, f32[8,8]{0,1:T(8,128)S(1)}) all-reduce(f32[8,8]{0,1:T(8,128)S(1)} %fusion.158, f32[8,8]{0,1:T(8,128)S(1)} %fusion.161), channel_id=1, replica_groups=mesh['row'=16,'col'=16] {'row','col'}, use_global_device_ids=true, to_apply=%region_10.14 | all-reduce | flops 128 | bytes 1024 | tf_op jit(solution)/shard_map/psum | solution.py:37
  1237.9 0.7 cholesky.81
  1238.7 0.6 compare_reduce_fusion
  1239.3 0.6 select_select_fusion
  1240.0 0.7 fusion.143
  1240.7 0.7 fusion.144
  1241.4 22.6 %subtract_divide_fusion = (f32[1,8]{1,0:T(1,128)S(1)}, f32[1,8]{1,0:T(1,128)S(1)}, f32[1,8]{1,0:T(1,128)S(1)}, f32[1,8]{1,0:T(1,128)S(1)}, f32[1,8]{1,0:T(1,128)...) fusion(f32[]{:T(128)} %bitcast.133, f32[]{:T(128)} %bitcast.132, f32[]{:T(128)} %bitcast.131, ...), kind=kLoop, calls=%fused_computation.183 | loop fusion | flops 512 | bytes 656 | tf_op jit(solution)/shard_map/div | solution.py:19
  1264.0 0.7 fusion.159
  1264.9 0.7 fusion.162
  (77 shorter events, 7.3 us)
Async XLA Ops:
  7.2 47.5 %copy-start.2 = (s32[1,1,2,128]{3,2,1,0:T(2,128)S(1)}, s32[1,1,2,128]{3,2,1,0:T(2,128)}, u32[]{:S(2)}) copy-start(s32[1,1,2,128]{3,2,1,0:T(2,128)} %param.12) | copy-start | bytes 3076
  7.2 110.3 %reduce-scatter.9.cloned.1.call-start = ((), (), s32[]{:S(2)}) async-start(), calls=%async_computation.7 | async-start | bytes 557056 | tf_op jit(solution)/shard_map/reduce_scatter | solution.py:105
  56.4 259.8 %reduce-scatter.7.cloned.1.call-start = ((), (), s32[]{:S(2)}) async-start(), calls=%async_computation.6 | async-start | bytes 557056 | tf_op jit(solution)/shard_map/reduce_scatter | solution.py:102
  84.2 6.3 copy-start.1
  84.2 6.4 copy-start
  90.4 448.7 %reduce-scatter.13.cloned.1.call-start = ((), (), s32[]{:S(2)}) async-start(), calls=%async_computation.9 | async-start | bytes 278528 | tf_op jit(solution)/shard_map/reduce_scatter | solution.py:105
  485.8 250.4 %reduce-scatter.11.cloned.1.call-start = ((), (), s32[]{:S(2)}) async-start(), calls=%async_computation.8 | async-start | bytes 278528 | tf_op jit(solution)/shard_map/reduce_scatter | solution.py:102
  492.5 466.9 %reduce-scatter.17.cloned.1.call-start = ((), (), s32[]{:S(2)}) async-start(), calls=%async_computation.11 | async-start | bytes 278528 | tf_op jit(solution)/shard_map/reduce_scatter | solution.py:105
  906.2 250.4 %reduce-scatter.15.cloned.1.call-start = ((), (), s32[]{:S(2)}) async-start(), calls=%async_computation.10 | async-start | bytes 278528 | tf_op jit(solution)/shard_map/reduce_scatter | solution.py:102
Sparse Core Ops, SparseCore 0:
  56.5 60.9 reduce-scatter.8
  121.8 194.3 reduce-scatter.6
  485.9 53.1 reduce-scatter.12
  543.3 192.9 reduce-scatter.10
  906.3 53.0 reduce-scatter.16
  963.5 193.0 reduce-scatter.14
where the time goes:
time: 1270 us
  waiting for transfers between devices  711 us (56%)
  blocking collectives  419 us (33%)
  other arithmetic  78.4 us (6%)
  matrix products  33.7 us (3%)
  local copies, waits for them, and re-layouts  15.6 us (1%)
  between operations  15.1 us (1%)
    reduce_scatter x3, waiting for transfers between devices, graph_product(): lax.psum_scatter(rows_total.reshape(width, row_span * tile_side), 'col',...  593 us
    psum x3, blocking collectives, gram_sums(): lax.psum((matmul_high(new_vecs, new_vecs.T), matmul_high(new_images, new_...  239 us
    reduce_scatter x3, waiting for transfers between devices, graph_product(): lax.psum_scatter(cols_total.reshape(width, col_span * tile_side), 'row',...  118 us
    all_gather x3, blocking collectives, graph_product(): row_side = lax.all_gather(short, 'col', axis=1, tiled=True)  103 us
    all_gather x3, blocking collectives, graph_product(): col_side = lax.all_gather(short, 'row', axis=1, tiled=True)  76.7 us
    div x3, other arithmetic, lower_inverse(): inverse_rows.append(partial_row / lower_factor[row_at, row_at])  67.8 us
  transfers between devices with their start and end apart: 6, of which 6 were waited for; matrix products, arithmetic and copies ran while one was open for 2% of the time, Pallas kernels for 0%

commit v1 on v0

--- a/solution.py
+++ b/solution.py
@@ -1,7 +1,17 @@
+import functools
 import jax
 import jax.numpy as jnp
 from jax import lax
 from jax.sharding import PartitionSpec as P
+
+
+def _settle_local_data(sheet, axis_tag, mesh_name):
+    for k0 in (axis_tag, mesh_name):
+        sheet = jax.lax.psum(sheet, k0)
+    return sheet
+
+
+choose_routes_all_in = functools.partial(_settle_local_data, axis_tag="col", mesh_name="row")
 
 
 def matmul_high(left, right):
@@ -34,8 +44,8 @@
 
 
 def gram_sums(new_vecs, new_images):
-    return lax.psum(
-        (matmul_high(new_vecs, new_vecs.T), matmul_high(new_images, new_vecs.T)), ("row", "col")
+    return choose_routes_all_in(
+        (matmul_high(new_vecs, new_vecs.T), matmul_high(new_images, new_vecs.T))
     )
 
 

time: 1270 us -> 1250 us (0.984)
  blocking collectives: 419 us -> 390 us
    psum x3 -> x6, blocking collectives: 239 us -> 218 us  [_settle_local_data(): sheet = jax.lax.psum(sheet, k0)]
where the time goes in v1:
time: 1250 us
  waiting for transfers between devices  714 us (57%)
  blocking collectives  390 us (31%)
  other arithmetic  78.4 us (6%)
  matrix products  33.7 us (3%)
  local copies, waits for them, and re-layouts  15.6 us (1%)
  between operations  15.2 us (1%)
    reduce_scatter x3, waiting for transfers between devices, graph_product(): lax.psum_scatter(rows_total.reshape(width, row_span * tile_side), 'col',...  593 us
    psum x6, blocking collectives, _settle_local_data(): sheet = jax.lax.psum(sheet, k0)  218 us
    reduce_scatter x3, waiting for transfers between devices, graph_product(): lax.psum_scatter(cols_total.reshape(width, col_span * tile_side), 'row',...  121 us
    all_gather x3, blocking collectives, graph_product(): row_side = lax.all_gather(short, 'col', axis=1, tiled=True)  98.2 us
    all_gather x3, blocking collectives, graph_product(): col_side = lax.all_gather(short, 'row', axis=1, tiled=True)  74.3 us
    div x3, other arithmetic, lower_inverse(): inverse_rows.append(partial_row / lower_factor[row_at, row_at])  67.8 us
  transfers between devices with their start and end apart: 6, of which 6 were waited for; matrix products, arithmetic and copies ran while one was open for 2% of the time, Pallas kernels for 0%

profile of v1, /device:TPU:1, one launch (start us, length us, event | category | flops | bytes accessed | tf_op | source)
XLA Modules:
  0.0 1247.0 jit_solution(7502663428791080272)
XLA Ops:
  7.2 0.8 compare_and_fusion
  8.0 0.8 slice_bitcast_fusion.2
  8.8 0.7 convert_convert_fusion
  9.5 0.7 multiply_convert_fusion
  10.2 39.4 %all_gather.19 = bf16[9,8192]{1,0:T(8,128)(2,1)S(1)} all-gather(bf16[9,512]{1,0:T(8,128)(2,1)S(1)} %pad_maximum_fusion.8), channel_id=1, replica_groups=mesh['row'=16,'col'=16] {'col'}, dimensions={1}, use_global_device_ids=true | all-gather | bytes 156672 | tf_op jit(solution)/shard_map/all_gather | solution.py:106
  50.5 0.7 gather_fusion.1
  51.2 3.4 fusion.8
  55.3 1.1 copy.34
  56.4 26.8 %all_gather.18 = bf16[9,8192]{1,0:T(8,128)(2,1)S(1)} all-gather(bf16[9,512]{1,0:T(8,128)(2,1)S(1)} %pad_maximum_fusion.8), channel_id=1, replica_groups=mesh['row'=16,'col'=16] {'row'}, dimensions={1}, use_global_device_ids=true | all-gather | bytes 156672 | tf_op jit(solution)/shard_map/all_gather | solution.py:105
  83.4 0.7 gather_fusion
  84.2 4.5 fusion.10
  89.3 1.1 copy.32
  90.7 26.9 %reduce-scatter.9.cloned.1.call-done = f32[9,512]{1,0:T(8,128)} async-done(((f32[9,8192]{1,0:T(8,128)}), f32[9,512]{1,0:T(8,128)}) %reduce-scatter.9.cloned.1.call-update) | async-done | bytes 18448 | tf_op jit(solution)/shard_map/reduce_scatter | solution.py:115
  117.5 198.7 %reduce-scatter.7.cloned.1.call-done = f32[9,512]{1,0:T(8,128)} async-done(((f32[9,8192]{1,0:T(8,128)}), f32[9,512]{1,0:T(8,128)}) %reduce-scatter.7.cloned.1.call-update) | async-done | bytes 18448 | tf_op jit(solution)/shard_map/reduce_scatter | solution.py:112
  316.2 0.8 add.112
  317.2 32.3 %all-reduce.2 = (f32[8,8]{0,1:T(8,128)S(1)}, f32[8,8]{0,1:T(8,128)S(1)}) all-reduce(f32[8,8]{0,1:T(8,128)S(1)} %fusion.95, f32[8,8]{0,1:T(8,128)S(1)} %fusion.87), channel_id=1, replica_groups=mesh['row'=16,'col'=16] {'col'}, use_global_device_ids=true, to_apply=%region_0.1 | all-reduce | flops 128 | bytes 1024 | tf_op jit(solution)/shard_map/psum | solution.py:10
  349.5 40.2 %all-reduce.5 = (f32[8,8]{0,1:T(8,128)S(1)}, f32[8,8]{0,1:T(8,128)S(1)}) all-reduce(f32[8,8]{0,1:T(8,128)S(1)} %get-tuple-element.9, f32[8,8]{0,1:T(8,128)S(1)} %get-tuple-element.10), channel_id=1, replica_groups=mesh['row'=16,'col'=16] {'row'}, use_global_device_ids=true, to_apply=%region_1.2 | all-reduce | flops 128 | bytes 1024 | tf_op jit(solution)/shard_map/psum | solution.py:10
  389.8 0.7 cholesky.59
  390.5 0.6 compare_reduce_fusion.2
  391.2 0.6 fusion.110
  391.8 0.7 fusion.147
  392.6 0.7 fusion.148
  393.3 22.6 %subtract_divide_fusion.14 = (f32[1,8]{1,0:T(1,128)S(1)}, f32[1,8]{1,0:T(1,128)S(1)}, f32[1,8]{1,0:T(1,128)S(1)}, f32[1,8]{1,0:T(1,128)S(1)}, f32[1,8]{1,0:T(1,1...) fusion(f32[]{:T(128)} %bitcast.36, f32[]{:T(128)} %bitcast.35, f32[]{:T(128)} %bitcast.34, ...), kind=kLoop, calls=%fused_computation.199 | loop fusion | flops 512 | bytes 656 | tf_op jit(solution)/shard_map/div | solution.py:29
  416.6 29.3 %all_gather.21 = bf16[8,8192]{1,0:T(8,128)(2,1)S(1)} all-gather(bf16[8,512]{1,0:T(8,128)(2,1)S(1)} %get-tuple-element.159), channel_id=1, replica_groups=mesh['row'=16,'col'=16] {'col'}, dimensions={1}, use_global_device_ids=true | all-gather | bytes 139264 | tf_op jit(solution)/shard_map/all_gather | solution.py:106
  445.9 23.8 %all_gather.20 = bf16[8,8192]{1,0:T(8,128)(2,1)S(1)} all-gather(bf16[8,512]{1,0:T(8,128)(2,1)S(1)} %get-tuple-element.159), channel_id=1, replica_groups=mesh['row'=16,'col'=16] {'row'}, dimensions={1}, use_global_device_ids=true | all-gather | bytes 139264 | tf_op jit(solution)/shard_map/all_gather | solution.py:105
  469.6 0.7 gather_fusion.3
  470.3 3.4 fusion.4
  474.2 0.8 copy.69
  475.1 0.7 gather_fusion.2
  475.8 4.5 fusion.6
  480.8 0.9 copy.70
  482.1 0.6 fusion.68
  482.8 47.1 %reduce-scatter.13.cloned.1.call-done = f32[8,512]{1,0:T(8,128)} async-done(((f32[8,8192]{1,0:T(8,128)}), f32[8,512]{1,0:T(8,128)}) %reduce-scatter.13.cloned.1.call-update) | async-done | bytes 16400 | tf_op jit(solution)/shard_map/reduce_scatter | solution.py:115
  529.9 197.1 %reduce-scatter.11.cloned.1.call-done = f32[8,512]{1,0:T(8,128)} async-done(((f32[8,8192]{1,0:T(8,128)}), f32[8,512]{1,0:T(8,128)}) %reduce-scatter.11.cloned.1.call-update) | async-done | bytes 16400 | tf_op jit(solution)/shard_map/reduce_scatter | solution.py:112
  727.0 0.7 subtract_multiply_fusion.1
  728.1 32.9 %all-reduce.1 = (f32[8,8]{0,1:T(8,128)S(1)}, f32[8,8]{0,1:T(8,128)S(1)}) all-reduce(f32[8,8]{0,1:T(8,128)S(1)} %fusion.152, f32[8,8]{0,1:T(8,128)S(1)} %fusion.155), channel_id=1, replica_groups=mesh['row'=16,'col'=16] {'col'}, use_global_device_ids=true, to_apply=%region_8.11 | all-reduce | flops 128 | bytes 1024 | tf_op jit(solution)/shard_map/psum | solution.py:10
  761.0 39.7 %all-reduce.4 = (f32[8,8]{0,1:T(8,128)S(1)}, f32[8,8]{0,1:T(8,128)S(1)}) all-reduce(f32[8,8]{0,1:T(8,128)S(1)} %get-tuple-element.7, f32[8,8]{0,1:T(8,128)S(1)} %get-tuple-element.8), channel_id=1, replica_groups=mesh['row'=16,'col'=16] {'row'}, use_global_device_ids=true, to_apply=%region_9.12 | all-reduce | flops 128 | bytes 1024 | tf_op jit(solution)/shard_map/psum | solution.py:10
  800.8 0.7 cholesky.70
  801.6 0.6 compare_reduce_fusion.1
  802.2 0.6 fusion.111
  802.9 0.7 fusion.145
  803.6 0.7 fusion.146
  804.3 22.6 %subtract_divide_fusion.7 = (f32[1,8]{1,0:T(1,128)S(1)}, f32[1,8]{1,0:T(1,128)S(1)}, f32[1,8]{1,0:T(1,128)S(1)}, f32[1,8]{1,0:T(1,128)S(1)}, f32[1,8]{1,0:T(1,12...) fusion(f32[]{:T(128)} %bitcast.87, f32[]{:T(128)} %bitcast.86, f32[]{:T(128)} %bitcast.85, ...), kind=kLoop, calls=%fused_computation.190 | loop fusion | flops 512 | bytes 656 | tf_op jit(solution)/shard_map/div | solution.py:29
  827.6 29.4 %all_gather.23 = bf16[8,8192]{1,0:T(8,128)(2,1)S(1)} all-gather(bf16[8,512]{1,0:T(8,128)(2,1)S(1)} %get-tuple-element.161), channel_id=1, replica_groups=mesh['row'=16,'col'=16] {'col'}, dimensions={1}, use_global_device_ids=true | all-gather | bytes 139264 | tf_op jit(solution)/shard_map/all_gather | solution.py:106
  857.1 23.8 %all_gather.22 = bf16[8,8192]{1,0:T(8,128)(2,1)S(1)} all-gather(bf16[8,512]{1,0:T(8,128)(2,1)S(1)} %get-tuple-element.161), channel_id=1, replica_groups=mesh['row'=16,'col'=16] {'row'}, dimensions={1}, use_global_device_ids=true | all-gather | bytes 139264 | tf_op jit(solution)/shard_map/all_gather | solution.py:105
  880.8 0.7 gather_fusion.5
  881.5 3.4 fusion
  885.4 0.8 copy.67
  886.3 0.7 gather_fusion.4
  887.0 4.5 fusion.2
  892.0 0.9 copy.68
  894.4 46.7 %reduce-scatter.17.cloned.1.call-done = f32[8,512]{1,0:T(8,128)} async-done(((f32[8,8192]{1,0:T(8,128)}), f32[8,512]{1,0:T(8,128)}) %reduce-scatter.17.cloned.1.call-update) | async-done | bytes 16400 | tf_op jit(solution)/shard_map/reduce_scatter | solution.py:115
  941.1 197.0 %reduce-scatter.15.cloned.1.call-done = f32[8,512]{1,0:T(8,128)} async-done(((f32[8,8192]{1,0:T(8,128)}), f32[8,512]{1,0:T(8,128)}) %reduce-scatter.15.cloned.1.call-update) | async-done | bytes 16400 | tf_op jit(solution)/shard_map/reduce_scatter | solution.py:112
  1138.1 0.7 subtract_multiply_fusion
  1139.7 32.9 %all-reduce = (f32[8,8]{0,1:T(8,128)S(1)}, f32[8,8]{0,1:T(8,128)S(1)}) all-reduce(f32[8,8]{0,1:T(8,128)S(1)} %fusion.158, f32[8,8]{0,1:T(8,128)S(1)} %fusion.161), channel_id=1, replica_groups=mesh['row'=16,'col'=16] {'col'}, use_global_device_ids=true, to_apply=%region_14.18 | all-reduce | flops 128 | bytes 1024 | tf_op jit(solution)/shard_map/psum | solution.py:10
  1172.6 39.7 %all-reduce.3 = (f32[8,8]{0,1:T(8,128)S(1)}, f32[8,8]{0,1:T(8,128)S(1)}) all-reduce(f32[8,8]{0,1:T(8,128)S(1)} %get-tuple-element.4, f32[8,8]{0,1:T(8,128)S(1)} %get-tuple-element.6), channel_id=1, replica_groups=mesh['row'=16,'col'=16] {'row'}, use_global_device_ids=true, to_apply=%region_15.19 | all-reduce | flops 128 | bytes 1024 | tf_op jit(solution)/shard_map/psum | solution.py:10
  1212.4 0.7 cholesky.81
  1213.1 0.6 compare_reduce_fusion
  1213.8 0.6 select_select_fusion
  1214.4 0.7 fusion.143
  1215.2 0.7 fusion.144
  1215.9 22.6 %subtract_divide_fusion = (f32[1,8]{1,0:T(1,128)S(1)}, f32[1,8]{1,0:T(1,128)S(1)}, f32[1,8]{1,0:T(1,128)S(1)}, f32[1,8]{1,0:T(1,128)S(1)}, f32[1,8]{1,0:T(1,128)...) fusion(f32[]{:T(128)} %bitcast.133, f32[]{:T(128)} %bitcast.132, f32[]{:T(128)} %bitcast.131, ...), kind=kLoop, calls=%fused_computation.183 | loop fusion | flops 512 | bytes 656 | tf_op jit(solution)/shard_map/div | solution.py:29
  1238.5 0.7 fusion.159
  1239.4 0.7 fusion.162
  (80 shorter events, 9.1 us)
Async XLA Ops:
  7.2 47.5 %copy-start.2 = (s32[1,1,2,128]{3,2,1,0:T(2,128)S(1)}, s32[1,1,2,128]{3,2,1,0:T(2,128)}, u32[]{:S(2)}) copy-start(s32[1,1,2,128]{3,2,1,0:T(2,128)} %param.12) | copy-start | bytes 3076
  7.2 110.4 %reduce-scatter.9.cloned.1.call-start = ((), (), s32[]{:S(2)}) async-start(), calls=%async_computation.7 | async-start | bytes 557056 | tf_op jit(solution)/shard_map/reduce_scatter | solution.py:115
  56.4 259.8 %reduce-scatter.7.cloned.1.call-start = ((), (), s32[]{:S(2)}) async-start(), calls=%async_computation.6 | async-start | bytes 557056 | tf_op jit(solution)/shard_map/reduce_scatter | solution.py:112
  84.1 6.4 copy-start.1
  84.2 6.4 copy-start
  90.4 439.5 %reduce-scatter.13.cloned.1.call-start = ((), (), s32[]{:S(2)}) async-start(), calls=%async_computation.9 | async-start | bytes 278528 | tf_op jit(solution)/shard_map/reduce_scatter | solution.py:115
  475.1 251.9 %reduce-scatter.11.cloned.1.call-start = ((), (), s32[]{:S(2)}) async-start(), calls=%async_computation.8 | async-start | bytes 278528 | tf_op jit(solution)/shard_map/reduce_scatter | solution.py:112
  481.8 459.3 %reduce-scatter.17.cloned.1.call-start = ((), (), s32[]{:S(2)}) async-start(), calls=%async_computation.11 | async-start | bytes 278528 | tf_op jit(solution)/shard_map/reduce_scatter | solution.py:115
  886.3 251.8 %reduce-scatter.15.cloned.1.call-start = ((), (), s32[]{:S(2)}) async-start(), calls=%async_computation.10 | async-start | bytes 278528 | tf_op jit(solution)/shard_map/reduce_scatter | solution.py:112
Sparse Core Ops, SparseCore 0:
  56.5 60.9 reduce-scatter.8
  121.8 194.3 reduce-scatter.6
  475.2 54.6 reduce-scatter.12
  534.0 192.9 reduce-scatter.10
  886.4 54.6 reduce-scatter.16
  945.2 192.7 reduce-scatter.14
